TPU v7x, 512 devices: a whole 4x4x16 slice. The times are simulated.
512 devices in a mesh: expert: 8 (over y, core), mp: 64 (over x, z).
Axes of the slice: x: 4, y: 4, z: 16, core: 2. Of those that a mesh axis runs over, the one named last changes fastest.
Arguments:
- context: bfloat16 [4096, 2048], P('expert', 'mp'), may hold values from -6 to 6
- out_proj: bfloat16 [2048, 2048], P('mp'), may hold values from -1 to 1, as said below
- routes: int32 [4096, 2], P('expert'), may hold values from 0 to 7, all different within a row; in each aligned block of 512 rows (0 to 511, 512 to 1023, ...) at most 256 rows name the same one
- router_logits: float32 [4096, 2], P('expert'), may hold values from -8 to 8
- w_gate: bfloat16 [45056, 2048], P('mp', 'expert'), may hold values from -0.125 to 0.125
- w_up: bfloat16 [45056, 2048], P('mp', 'expert'), may hold values from -0.125 to 0.125
- w_down: bfloat16 [45056, 2048], P('mp', 'expert'), may hold values from -0.078125 to 0.078125
- norm_gain: float32 [2048], P('mp'), may hold values from 0.25 to 1.75
- request_order: int32 [4096], P('expert'), may hold values from 0 to 4095, each once
Outputs:
- restored: bfloat16 [4096, 2048], P('expert', 'mp')
Inputs may be any that keep to these rules, and one draw needn't show every extreme that they name: `routes`: each row names 2 different experts. Within each aligned block of 512 rows no expert is named by more than 256 rows, and in some blocks one expert is named by exactly 256 rows. `request_order`: A permutation of the 4096 token rows. `out_proj`: entries of the order of one over the square root of 2048.
All inputs are finite; a program needn't handle non-finite values.
Results may differ from a plain program's by a relative error of at most 0.0056.
Values may be sent and summed in bfloat16 or wider, within the bound.
No kernel may reach another device: no remote copies, remote signals or barrier semaphores. Data moves between devices by JAX's collectives and lax.ppermute only.
A program may use at most 64 MiB of HBM per device.

v0:
```python
import jax
import jax.numpy as jnp
from jax import lax
from jax.sharding import PartitionSpec as P

EXPERTS = 8
CAP = 256
epsilon = 1e-06


def slot_targets(routes, capacity, experts):
    flat_routes = routes.reshape(-1)
    onehot = (flat_routes[:, None] == jnp.arange(experts, dtype=jnp.int32)[None, :]).astype(
        jnp.int32
    )
    earlier = jnp.cumsum(onehot, axis=0) - onehot
    slot_index = jnp.sum(earlier * onehot, axis=1)
    return flat_routes * capacity + slot_index


def shards(
    context, out_proj, routes, router_logits, w_gate, w_up, w_down, norm_gain, request_order
):
    tok_rows = context.shape[0]
    feat_local = context.shape[1]
    model_width = out_proj.shape[1]
    mp_count = lax.axis_size("mp")
    copies = mp_count // EXPERTS
    capacity = CAP
    top_k = routes.shape[1]
    attended = jnp.einsum(
        "td,cd->tc",
        lax.all_gather(context, "mp", axis=1, tiled=True),
        out_proj,
        preferred_element_type=jnp.float32,
    ).astype(jnp.bfloat16)
    destination = slot_targets(routes, capacity, EXPERTS)
    source_rows = jnp.repeat(jnp.arange(tok_rows, dtype=jnp.int32), top_k)
    slotted = (
        jnp.zeros((EXPERTS * capacity, feat_local), jnp.bfloat16)
        .at[destination]
        .set(attended[source_rows])
    )
    slotted = jnp.repeat(slotted.reshape(EXPERTS, capacity, feat_local), copies, axis=0)
    outgoing = slotted.transpose(1, 0, 2).reshape(capacity, mp_count * feat_local)
    inbox_rows = lax.all_to_all(outgoing, "mp", split_axis=1, concat_axis=1, tiled=True)
    gate_next = jnp.einsum(
        "rd,hd->rh",
        inbox_rows,
        lax.all_gather(w_gate, "expert", axis=1, tiled=True),
        preferred_element_type=jnp.float32,
    )
    up_next = jnp.einsum(
        "rd,hd->rh",
        inbox_rows,
        lax.all_gather(w_up, "expert", axis=1, tiled=True),
        preferred_element_type=jnp.float32,
    )
    activated = (jax.nn.silu(gate_next) * up_next).astype(jnp.bfloat16)
    partial_value = jnp.dot(
        activated,
        lax.all_gather(w_down, "expert", axis=1, tiled=True),
        preferred_element_type=jnp.float32,
    )
    returned = lax.all_to_all(partial_value, "mp", split_axis=1, concat_axis=0, tiled=True)
    expert_out = jnp.sum(returned.reshape(EXPERTS, copies, capacity, feat_local), axis=1).reshape(
        EXPERTS * capacity, feat_local
    )
    picked = expert_out[destination].reshape(tok_rows, top_k, feat_local)
    weights = 1.0 / (1.0 + jnp.exp(router_logits[:, ::-1] - router_logits))
    branch = jnp.sum(picked * weights[:, :, None], axis=1)
    combined = attended.astype(jnp.float32) + branch
    squares = lax.psum(jnp.sum(combined * combined, axis=1), "mp")
    normed = (
        combined * norm_gain[None, :] * lax.rsqrt(squares / model_width + epsilon)[:, None]
    ).astype(jnp.bfloat16)
    everyone = lax.all_gather(normed, "expert", axis=0, tiled=True)
    return everyone[request_order]


def solution(mesh):
    placed = (
        P("expert", "mp"),
        P("mp", None),
        P("expert", None),
        P("expert", None),
        P("mp", "expert"),
        P("mp", "expert"),
        P("mp", "expert"),
        P("mp"),
        P("expert"),
    )
    return jax.shard_map(
        shards, mesh=mesh, in_specs=placed, out_specs=P("expert", "mp"), check_vma=False
    )
```

profile of v0, /device:TPU:1, one launch (start us, length us, event | category | flops | bytes accessed | tf_op | source)
XLA Modules:
  0.0 565.7 jit_solution(14208333560372502879)
XLA Ops:
  6.5 0.0 copy-start
  6.5 0.7 all-gather.5.cloned.1.call-update
  7.3 0.0 all-gather.7.cloned.1.call-start
  7.3 0.7 all-gather.7.cloned.1.call-update
  8.0 0.0 all-gather.11.cloned.1.call-start
  8.1 0.7 all-gather.11.cloned.1.call-update
  8.7 0.0 all-gather.9.cloned.1.call-start
  8.8 0.5 all-gather.9.cloned.1.call-update
  9.3 0.8 copy.42
  10.2 0.2 eq.29
  10.3 0.2 eq.25
  10.5 0.7 broadcast_multiply_fusion
  11.2 2.3 reduce-window.6
  13.5 0.3 slice_reduce_fusion
  13.7 0.2 reduce-window.9
  13.9 0.1 add_bitcast_fusion
  14.0 0.2 copy.41
  14.1 0.2 mul.55
  14.4 0.2 reshape.104
  14.6 133.1 %all-gather.5.cloned.1.call-done = bf16[512,2048]{0,1:T(8,128)(2,1)} async-done(((bf16[512,32]{0,1:T(8,128)(2,1)}), bf16[512,2048]{0,1:T(8,128)(2,1)}) %all-gather.5.cloned.1.call-update) | async-done | bytes 2097168 | tf_op jit(solution)/shard_map/all_gather | solution.py:33
  147.7 2.0 convolution_convert_fusion
  149.7 0.1 copy.44
  149.9 6.4 %scatter_custom_fusion = bf16[2048,32]{1,0:T(8,128)(2,1)S(1)} fusion(s32[1024]{0:T(1024)S(1)} %bitcast.48, bf16[512,32]{1,0:T(8,128)(2,1)S(1)} %copy.44, s32[1024]{0:T(1024)S(1)} %broadcast_clamp_fusion.1, bf16[]{:T(256)} %constant.10.clone.1), kind=kCustom, calls=%fused_computation.16 | custom fusion | bytes 131074 | tf_op jit(solution)/shard_map/scatter | solution.py:42
  156.3 0.2 copy.46
  156.5 1.2 broadcast_in_dim.10
  157.7 8.8 %all-to-all-start = ((bf16[256,64,32]{0,2,1:T(8,128)(2,1)}), bf16[256,64,32]{0,2,1:T(8,128)(2,1)S(1)}, u32[]{:S(2)}, u32[]{:S(2)}) async-start(bf16[256,64,32]{0,2,1:T(8,128)(2,1)} %bitcast.6), calls=%async_computation | async-start | bytes 2097152 | tf_op jit(solution)/shard_map/all_to_all | solution.py:46
  166.5 26.9 %all-gather.7.cloned.1.call-done = bf16[704,2048]{1,0:T(8,128)(2,1)} async-done(((bf16[704,256]{1,0:T(8,128)(2,1)}), bf16[704,2048]{1,0:T(8,128)(2,1)}) %all-gather.7.cloned.1.call-update) | async-done | bytes 2883600 | tf_op jit(solution)/shard_map/all_gather | solution.py:50
  193.4 12.3 %all-to-all-done = bf16[256,64,32]{0,2,1:T(8,128)(2,1)S(1)} async-done(((bf16[256,64,32]{0,2,1:T(8,128)(2,1)}), bf16[256,64,32]{0,2,1:T(8,128)(2,1)S(1)}, u32[]{:S(2)}, u32[]{:S(2)}) %all-to-all-start) | async-done | bytes 1048608 | tf_op jit(solution)/shard_map/all_to_all | solution.py:46
  205.6 2.7 fusion.16
  208.4 26.4 %all-gather.11.cloned.1.call-done = bf16[704,2048]{1,0:T(8,128)(2,1)} async-done(((bf16[704,256]{1,0:T(8,128)(2,1)}), bf16[704,2048]{1,0:T(8,128)(2,1)}) %all-gather.11.cloned.1.call-update) | async-done | bytes 2883600 | tf_op jit(solution)/shard_map/all_gather | solution.py:62
  234.8 41.3 %all-gather.9.cloned.1.call-done = bf16[704,2048]{1,0:T(8,128)(2,1)} async-done(((bf16[704,256]{1,0:T(8,128)(2,1)}), bf16[704,2048]{1,0:T(8,128)(2,1)}) %all-gather.9.cloned.1.call-update) | async-done | bytes 2883600 | tf_op jit(solution)/shard_map/all_gather | solution.py:56
  276.1 7.2 %fusion.1 = f32[256,2048]{0,1:T(8,128)} fusion(bf16[704,2048]{1,0:T(8,128)(2,1)} %all-gather.11.cloned.1.call-done, bf16[704,2048]{1,0:T(8,128)(2,1)} %all-gather.9.cloned.1.call-done, bf16[256,2048]{0,1:T(8,128)(2,1)S(1)} %bitcast.46, f32[256,704]{0,1:T(8,128)S(1)} %fusion.16), kind=kOutput, calls=%fused_computation.8 | convolution fusion | flops 1477476352 | bytes 9633792 | tf_op jit(solution)/shard_map/dot_general | solution.py:60
  283.4 15.6 %all-to-all-start.1 = ((f32[256,64,32]{0,2,1:T(8,128)}), f32[256,64,32]{0,2,1:T(8,128)S(1)}, u32[]{:S(2)}, u32[]{:S(2)}) async-start(f32[256,64,32]{0,2,1:T(8,128)} %bitcast.43), calls=%async_computation.1 | async-start | bytes 4194304 | tf_op jit(solution)/shard_map/all_to_all | solution.py:65
  299.0 0.1 rev.3
  299.2 0.1 copy.49
  299.4 91.4 %all-to-all-done.1 = f32[256,64,32]{0,2,1:T(8,128)S(1)} async-done(((f32[256,64,32]{0,2,1:T(8,128)}), f32[256,64,32]{0,2,1:T(8,128)S(1)}, u32[]{:S(2)}, u32[]{:S(2)}) %all-to-all-start.1) | async-done | bytes 2097184 | tf_op jit(solution)/shard_map/all_to_all | solution.py:65
  390.8 0.2 bitcast_reduce_fusion
  390.9 0.3 copy.48
  391.3 0.0 copy-start.3
  391.3 2.8 gather_fusion
  394.1 2.8 multiply_reduce_fusion
  396.9 0.1 copy.50
  397.1 118.5 %psum.7 = f32[512]{0:T(512)S(1)} all-reduce(f32[512]{0:T(512)S(1)} %multiply_reduce_fusion.1), channel_id=1, replica_groups=mesh['expert'=8,'mp'=64] {'mp'}, use_global_device_ids=true, to_apply=%region_7.8 | all-reduce | flops 512 | bytes 4096 | tf_op jit(solution)/shard_map/psum | solution.py:73
  515.6 0.1 multiply_convert_fusion
  515.6 41.0 %all_gather.19 = bf16[4096,32]{0,1:T(8,128)(2,1)S(1)} all-gather(bf16[512,32]{0,1:T(8,128)(2,1)S(1)} %multiply_convert_fusion), channel_id=1, replica_groups=mesh['expert'=8,'mp'=64] {'expert'}, dimensions={0}, use_global_device_ids=true | all-gather | bytes 294912 | tf_op jit(solution)/shard_map/all_gather | solution.py:77
  556.6 0.5 copy.51
  557.1 1.3 gather_fusion.1
  558.4 0.7 copy.52
  (19 shorter events, 0.2 us)
Async XLA Ops:
  6.5 141.2 %copy-start = (bf16[32,2048]{1,0:T(8,128)(2,1)S(1)}, bf16[32,2048]{1,0:T(8,128)(2,1)}, u32[]{:S(2)}) copy-start(bf16[32,2048]{1,0:T(8,128)(2,1)} %param.10) | copy-start | bytes 393220
  6.5 141.2 %all-gather.5.cloned.1.call-start = ((), (), s32[]{:S(2)}) async-start(), calls=%async_computation.2 | async-start | bytes 2129920 | tf_op jit(solution)/shard_map/all_gather | solution.py:33
  7.3 186.1 %all-gather.7.cloned.1.call-start = ((), (), s32[]{:S(2)}) async-start(), calls=%async_computation.3 | async-start | bytes 3244032 | tf_op jit(solution)/shard_map/all_gather | solution.py:50
  8.0 226.8 %all-gather.11.cloned.1.call-start = ((), (), s32[]{:S(2)}) async-start(), calls=%async_computation.5 | async-start | bytes 3244032 | tf_op jit(solution)/shard_map/all_gather | solution.py:62
  8.7 267.4 %all-gather.9.cloned.1.call-start = ((), (), s32[]{:S(2)}) async-start(), calls=%async_computation.4 | async-start | bytes 3244032 | tf_op jit(solution)/shard_map/all_gather | solution.py:56
  157.7 48.0 %all-to-all-start = ((bf16[256,64,32]{0,2,1:T(8,128)(2,1)}), bf16[256,64,32]{0,2,1:T(8,128)(2,1)S(1)}, u32[]{:S(2)}, u32[]{:S(2)}) async-start(bf16[256,64,32]{0,2,1:T(8,128)(2,1)} %bitcast.6), calls=%async_computation | async-start | bytes 2097152 | tf_op jit(solution)/shard_map/all_to_all | solution.py:46
  283.4 15.7 %copy-start.1 = (f32[512,2]{0,1:T(2,128)S(1)}, f32[512,2]{0,1:T(2,128)}, u32[]{:S(2)}) copy-start(f32[512,2]{0,1:T(2,128)} %param.12) | copy-start | bytes 12292
  283.4 16.0 %copy-start.2 = (s32[512]{0:T(512)S(1)}, s32[512]{0:T(512)}, u32[]{:S(2)}) copy-start(s32[512]{0:T(512)} %param.17) | copy-start | bytes 6148
  283.4 107.4 %all-to-all-start.1 = ((f32[256,64,32]{0,2,1:T(8,128)}), f32[256,64,32]{0,2,1:T(8,128)S(1)}, u32[]{:S(2)}, u32[]{:S(2)}) async-start(f32[256,64,32]{0,2,1:T(8,128)} %bitcast.43), calls=%async_computation.1 | async-start | bytes 4194304 | tf_op jit(solution)/shard_map/all_to_all | solution.py:65
  391.3 124.3 %copy-start.3 = (f32[32]{0:T(128)S(1)}, f32[32]{0:T(128)}, u32[]{:S(2)}) copy-start(f32[32]{0:T(128)} %param.16) | copy-start | bytes 388
Sparse Core Ops, SparseCore 0:
  10.3 137.3 all-gather.4
  149.8 43.5 all-gather.6
  195.5 39.2 all-gather.10
  236.8 39.2 all-gather.8
where the time goes:
time: 566 us
  waiting for transfers between devices  334 us (59%)
  blocking collectives  159 us (28%)
  starting transfers between devices  24.5 us (4%)
  local copies, waits for them, and re-layouts  16 us (3%)
  between operations  13.4 us (2%)
  matrix products  12 us (2%)
  other arithmetic  6.35 us (1%)
    all_gather x1, waiting for transfers between devices, shards(): lax.all_gather(context, 'mp', axis=1, tiled=True)  133 us
    psum x1, blocking collectives, shards(): squares = lax.psum(jnp.sum(combined * combined, axis=1), 'mp')  118 us
    all_to_all x1, waiting for transfers between devices, shards(): lax.all_to_all(partial_value, 'mp', split_axis=1, concat_axis=0, tiled=True)  91.4 us
    all_gather x1, waiting for transfers between devices, shards(): lax.all_gather(w_up, 'expert', axis=1, tiled=True)  41.3 us
    all_gather x1, blocking collectives, shards(): everyone = lax.all_gather(normed, 'expert', axis=0, tiled=True)  41 us
    all_gather x1, waiting for transfers between devices, shards(): lax.all_gather(w_gate, 'expert', axis=1, tiled=True)  26.9 us
    all_gather x1, waiting for transfers between devices, shards(): lax.all_gather(w_down, 'expert', axis=1, tiled=True)  26.4 us
    all_to_all x1, starting transfers between devices, shards(): lax.all_to_all(partial_value, 'mp', split_axis=1, concat_axis=0, tiled=True)  15.6 us
  transfers between devices with their start and end apart: 6, of which 6 were waited for; matrix products, arithmetic and copies ran while one was open for 3% of the time, Pallas kernels for 0%

commit v1 on v0

--- a/solution.py
+++ b/solution.py
@@ -59,7 +59,9 @@
     activated = (jax.nn.silu(gate_next) * up_next).astype(jnp.bfloat16)
     partial_value = jnp.dot(
         activated,
-        lax.all_gather(w_down, "expert", axis=1, tiled=True),
+        jnp.concatenate(
+            lax.all_to_all(jnp.stack([w_down] * lax.axis_size("expert")), "expert", 0, 0), axis=1
+        ),
         preferred_element_type=jnp.float32,
     )
     returned = lax.all_to_all(partial_value, "mp", split_axis=1, concat_axis=0, tiled=True)

time: 566 us -> 525 us (0.928)
  waiting for transfers between devices: 334 us -> 269 us
  local copies, waits for them, and re-layouts: 16 us -> 28.3 us
  starting transfers between devices: 24.5 us -> 35.3 us
    all_gather x1 -> x0, waiting for transfers between devices: 26.4 us -> none  [shards(): lax.all_gather(w_down, 'expert', axis=1, tiled=True)]
    all_gather x1, waiting for transfers between devices: 41.3 us -> 20 us  [shards(): lax.all_gather(w_up, 'expert', axis=1, tiled=True)]
    all_gather x1, waiting for transfers between devices: 133 us -> 122 us  [shards(): lax.all_gather(context, 'mp', axis=1, tiled=True)]
    all_to_all x0 -> x1, starting transfers between devices: none -> 10.5 us  [shards(): lax.all_to_all(jnp.stack([w_down] * lax.axis_size('expert')), 'expert', 0...]
    all_gather x1, waiting for transfers between devices: 26.9 us -> 16.4 us  [shards(): lax.all_gather(w_gate, 'expert', axis=1, tiled=True)]
  transfers between devices with their start and end apart: 6 -> 6, of which waited for: 6 -> 5; matrix products, arithmetic and copies ran while one was open for 3% -> 6% of each run, Pallas kernels for 0% -> 0%
where the time goes in v1:
time: 525 us; the launch traced here: 524 us
  waiting for transfers between devices  269 us (51%)
  blocking collectives  159 us (30%)
  starting transfers between devices  35.3 us (7%)
  local copies, waits for them, and re-layouts  28.3 us (5%)
  between operations  13.3 us (3%)
  matrix products  12.9 us (2%)
  other arithmetic  5.67 us (1%)
    all_gather x1, waiting for transfers between devices, shards(): lax.all_gather(context, 'mp', axis=1, tiled=True)  122 us
    psum x1, blocking collectives, shards(): squares = lax.psum(jnp.sum(combined * combined, axis=1), 'mp')  118 us
    all_to_all x1, waiting for transfers between devices, shards(): lax.all_to_all(partial_value, 'mp', split_axis=1, concat_axis=0, tiled=True)  91.4 us
    all_gather x1, blocking collectives, shards(): everyone = lax.all_gather(normed, 'expert', axis=0, tiled=True)  41 us
    all_gather x1, waiting for transfers between devices, shards(): lax.all_gather(w_up, 'expert', axis=1, tiled=True)  20 us
    all_to_all x1, waiting for transfers between devices, shards(): lax.all_to_all(outgoing, 'mp', split_axis=1, concat_axis=1, tiled=True)  17.5 us
    all_gather x1, waiting for transfers between devices, shards(): lax.all_gather(w_gate, 'expert', axis=1, tiled=True)  16.4 us
    all_to_all x1, starting transfers between devices, shards(): lax.all_to_all(partial_value, 'mp', split_axis=1, concat_axis=0, tiled=True)  15.6 us
  transfers between devices with their start and end apart: 6, of which 5 were waited for; matrix products, arithmetic and copies ran while one was open for 6% of the time, Pallas kernels for 0%

profile of v1, /device:TPU:1, one launch (start us, length us, event | category | flops | bytes accessed | tf_op | source)
XLA Modules:
  0.0 524.1 jit_solution(7279656313269970555)
XLA Ops:
  6.5 0.7 all-gather.4.cloned.1.call-update
  7.3 0.0 all-gather.6.cloned.1.call-start
  7.3 0.7 all-gather.6.cloned.1.call-update
  8.0 2.7 stack.2
  10.8 10.5 %all-to-all-start.1 = ((bf16[8,704,256]{2,1,0:T(8,128)(2,1)}), bf16[8,704,256]{2,1,0:T(8,128)(2,1)S(1)}, u32[]{:S(2)}, u32[]{:S(2)}) async-start(bf16[8,704,256]{2,1,0:T(8,128)(2,1)} %stack.2), calls=%async_computation.1 | async-start | bytes 5767168 | tf_op jit(solution)/shard_map/all_to_all | solution.py:63
  21.3 0.7 all-gather.8.cloned.1.call-update
  22.0 0.1 copy.45
  22.2 0.2 eq.29
  22.4 0.2 eq.25
  22.5 2.3 reduce-window.6
  24.8 0.3 slice_reduce_fusion
  25.1 0.2 reduce-window.9
  25.3 0.2 copy.44
  25.4 0.2 mul.55
  25.6 0.2 reshape.113
  25.8 0.1 add_bitcast_fusion
  26.0 121.7 %all-gather.4.cloned.1.call-done = bf16[512,2048]{0,1:T(8,128)(2,1)} async-done(((bf16[512,32]{0,1:T(8,128)(2,1)}), bf16[512,2048]{0,1:T(8,128)(2,1)}) %all-gather.4.cloned.1.call-update) | async-done | bytes 2097168 | tf_op jit(solution)/shard_map/all_gather | solution.py:33
  147.7 2.0 convolution_convert_fusion
  149.8 0.8 copy.47
  150.5 9.5 %scatter_custom_fusion = bf16[2048,32]{1,0:T(8,128)(2,1)S(1)} fusion(s32[1024]{0:T(1024)S(1)} %bitcast.69, bf16[512,32]{1,0:T(8,128)(2,1)} %copy.47, s32[1024]{0:T(1024)S(1)} %broadcast_clamp_fusion.1, bf16[]{:T(256)} %constant.10.clone.1), kind=kCustom, calls=%fused_computation.10 | custom fusion | bytes 131584 | tf_op jit(solution)/shard_map/scatter | solution.py:42
  160.0 0.8 copy.49
  160.8 0.0 all-to-all-done.1
  160.8 2.0 broadcast_in_dim.10
  162.8 9.0 %all-to-all-start = ((bf16[256,64,32]{0,2,1:T(8,128)(2,1)}), bf16[256,64,32]{0,2,1:T(8,128)(2,1)}, u32[]{:S(2)}, u32[]{:S(2)}) async-start(bf16[256,64,32]{0,2,1:T(8,128)(2,1)} %bitcast.64), calls=%async_computation | async-start | bytes 2097152 | tf_op jit(solution)/shard_map/all_to_all | solution.py:46
  171.9 2.0 copy.66
  173.9 3.1 copy.51
  177.0 16.4 %all-gather.6.cloned.1.call-done = bf16[704,2048]{1,0:T(8,128)(2,1)} async-done(((bf16[704,256]{1,0:T(8,128)(2,1)}), bf16[704,2048]{1,0:T(8,128)(2,1)}) %all-gather.6.cloned.1.call-update) | async-done | bytes 2883600 | tf_op jit(solution)/shard_map/all_gather | solution.py:50
  193.4 17.5 %all-to-all-done = bf16[256,64,32]{0,2,1:T(8,128)(2,1)} async-done(((bf16[256,64,32]{0,2,1:T(8,128)(2,1)}), bf16[256,64,32]{0,2,1:T(8,128)(2,1)}, u32[]{:S(2)}, u32[]{:S(2)}) %all-to-all-start) | async-done | bytes 1048608 | tf_op jit(solution)/shard_map/all_to_all | solution.py:46
  210.9 3.9 fusion.10
  214.8 20.0 %all-gather.8.cloned.1.call-done = bf16[704,2048]{1,0:T(8,128)(2,1)} async-done(((bf16[704,256]{1,0:T(8,128)(2,1)}), bf16[704,2048]{1,0:T(8,128)(2,1)}) %all-gather.8.cloned.1.call-update) | async-done | bytes 2883600 | tf_op jit(solution)/shard_map/all_gather | solution.py:56
  234.8 6.9 %fusion.9 = f32[256,64,32]{0,2,1:T(8,128)} fusion(bf16[64,32,704]{2,1,0:T(8,128)(2,1)S(1)} %bitcast.65, bf16[704,2048]{1,0:T(8,128)(2,1)} %all-gather.8.cloned.1.call-done, bf16[256,2048]{0,1:T(8,128)(2,1)} %bitcast.7, f32[256,704]{0,1:T(8,128)} %fusion.10), kind=kOutput, calls=%fused_computation.34 | convolution fusion | flops 1477476352 | bytes 9633792 | tf_op jit(solution)/shard_map/dot_general | solution.py:60
  241.7 15.6 %all-to-all-start.2 = ((f32[256,64,32]{0,2,1:T(8,128)}), f32[256,64,32]{0,2,1:T(8,128)S(1)}, u32[]{:S(2)}, u32[]{:S(2)}) async-start(f32[256,64,32]{0,2,1:T(8,128)} %fusion.9), calls=%async_computation.2 | async-start | bytes 4194304 | tf_op jit(solution)/shard_map/all_to_all | solution.py:67
  257.4 0.1 rev.3
  257.5 0.1 copy.56
  257.7 91.4 %all-to-all-done.2 = f32[256,64,32]{0,2,1:T(8,128)S(1)} async-done(((f32[256,64,32]{0,2,1:T(8,128)}), f32[256,64,32]{0,2,1:T(8,128)S(1)}, u32[]{:S(2)}, u32[]{:S(2)}) %all-to-all-start.2) | async-done | bytes 2097184 | tf_op jit(solution)/shard_map/all_to_all | solution.py:67
  349.1 0.2 bitcast_reduce_fusion
  349.3 0.3 copy.55
  349.6 0.0 copy-start.2
  349.7 0.0 copy-start.6
  349.7 2.8 gather_fusion
  352.5 2.8 multiply_reduce_fusion
  355.3 0.1 copy.57
  355.4 118.5 %psum.7 = f32[512]{0:T(512)S(1)} all-reduce(f32[512]{0:T(512)S(1)} %multiply_reduce_fusion.1), channel_id=1, replica_groups=mesh['expert'=8,'mp'=64] {'mp'}, use_global_device_ids=true, to_apply=%region_7.8 | all-reduce | flops 512 | bytes 4096 | tf_op jit(solution)/shard_map/psum | solution.py:75
  473.9 0.1 multiply_convert_fusion
  474.0 41.0 %all_gather.15 = bf16[4096,32]{0,1:T(8,128)(2,1)S(1)} all-gather(bf16[512,32]{0,1:T(8,128)(2,1)S(1)} %multiply_convert_fusion), channel_id=1, replica_groups=mesh['expert'=8,'mp'=64] {'expert'}, dimensions={0}, use_global_device_ids=true | all-gather | bytes 294912 | tf_op jit(solution)/shard_map/all_gather | solution.py:79
  515.0 0.5 copy.58
  515.5 1.3 gather_fusion.1
  516.8 0.7 copy.59
  (27 shorter events, 0.2 us)
Async XLA Ops:
  6.5 141.2 %copy-start = (bf16[32,2048]{1,0:T(8,128)(2,1)S(1)}, bf16[32,2048]{1,0:T(8,128)(2,1)}, u32[]{:S(2)}) copy-start(bf16[32,2048]{1,0:T(8,128)(2,1)} %param.10) | copy-start | bytes 393220
  6.5 141.2 %all-gather.4.cloned.1.call-start = ((), (), s32[]{:S(2)}) async-start(), calls=%async_computation.3 | async-start | bytes 2129920 | tf_op jit(solution)/shard_map/all_gather | solution.py:33
  7.3 186.1 %all-gather.6.cloned.1.call-start = ((), (), s32[]{:S(2)}) async-start(), calls=%async_computation.4 | async-start | bytes 3244032 | tf_op jit(solution)/shard_map/all_gather | solution.py:50
  10.8 11.3 %copy-start.3 = (s32[512,2]{0,1:T(2,128)S(1)}, s32[512,2]{0,1:T(2,128)}, u32[]{:S(2)}) copy-start(s32[512,2]{0,1:T(2,128)} %param.11) | copy-start | bytes 12292
  10.8 150.1 %all-to-all-start.1 = ((bf16[8,704,256]{2,1,0:T(8,128)(2,1)}), bf16[8,704,256]{2,1,0:T(8,128)(2,1)S(1)}, u32[]{:S(2)}, u32[]{:S(2)}) async-start(bf16[8,704,256]{2,1,0:T(8,128)(2,1)} %stack.2), calls=%async_computation.1 | async-start | bytes 5767168 | tf_op jit(solution)/shard_map/all_to_all | solution.py:63
  21.3 213.5 %all-gather.8.cloned.1.call-start = ((), (), s32[]{:S(2)}) async-start(), calls=%async_computation.5 | async-start | bytes 3244032 | tf_op jit(solution)/shard_map/all_gather | solution.py:56
  149.7 0.8 copy-start.1
  162.8 48.0 %all-to-all-start = ((bf16[256,64,32]{0,2,1:T(8,128)(2,1)}), bf16[256,64,32]{0,2,1:T(8,128)(2,1)}, u32[]{:S(2)}, u32[]{:S(2)}) async-start(bf16[256,64,32]{0,2,1:T(8,128)(2,1)} %bitcast.64), calls=%async_computation | async-start | bytes 2097152 | tf_op jit(solution)/shard_map/all_to_all | solution.py:46
  241.7 15.7 %copy-start.4 = (f32[512,2]{0,1:T(2,128)S(1)}, f32[512,2]{0,1:T(2,128)}, u32[]{:S(2)}) copy-start(f32[512,2]{0,1:T(2,128)} %param.12) | copy-start | bytes 12292
  241.7 16.0 %copy-start.5 = (s32[512]{0:T(512)S(1)}, s32[512]{0:T(512)}, u32[]{:S(2)}) copy-start(s32[512]{0:T(512)} %param.17) | copy-start | bytes 6148
  241.7 107.4 %all-to-all-start.2 = ((f32[256,64,32]{0,2,1:T(8,128)}), f32[256,64,32]{0,2,1:T(8,128)S(1)}, u32[]{:S(2)}, u32[]{:S(2)}) async-start(f32[256,64,32]{0,2,1:T(8,128)} %fusion.9), calls=%async_computation.2 | async-start | bytes 4194304 | tf_op jit(solution)/shard_map/all_to_all | solution.py:67
  349.6 5.8 %copy-start.2 = (bf16[512,32]{0,1:T(8,128)(2,1)S(1)}, bf16[512,32]{0,1:T(8,128)(2,1)}, u32[]{:S(2)}) copy-start(bf16[512,32]{0,1:T(8,128)(2,1)} %copy-done.1) | copy-start | bytes 98308
  349.7 124.3 %copy-start.6 = (f32[32]{0:T(128)S(1)}, f32[32]{0:T(128)}, u32[]{:S(2)}) copy-start(f32[32]{0:T(128)} %param.16) | copy-start | bytes 388
Sparse Core Ops, SparseCore 0:
  10.3 137.3 all-gather.3
  149.8 43.5 all-gather.5
  195.5 39.2 all-gather.7
